TPU v7x, 256 devices: a whole 4x4x8 slice. The times are simulated.
256 devices in a mesh: pair: 32 (over y, x, core), lam: 8 (over z).
Axes of the slice: x: 4, y: 4, z: 8, core: 2. Of those that a mesh axis runs over, the one named last changes fastest.
Arguments:
- integrals: bfloat16 [32, 64, 4, 64, 1024], P('pair', 'lam'), may hold values from -0.119628906 to 0.119628906
- tile_pair: int32 [32, 64], P('pair', 'lam'), may hold values from 0 to 15, as said below
- tile_lam: int32 [32, 64], P('pair', 'lam'), may hold values from 0 to 15, as said below
- tile_count: int32 [32, 8], P('pair', 'lam'), may hold values from 1 to 8, as said below
- mu_index: int32 [2048], P('pair'), may hold values from 0 to 1023
- nu_index: int32 [2048], P('pair'), may hold values from 0 to 1023
- occupied_coef: bfloat16 [1024, 16], replicated, may hold values from -1.5 to 1.5
- virtual_coef: bfloat16 [1024, 1280], replicated, may hold values from -1.5 to 1.5
Outputs:
- orbital_integrals: float32 [16, 1280, 20480], P('lam', 'pair')
Inputs may be any that keep to these rules, and one draw needn't show every extreme that they name: On every device the live and dead slots name distinct pairs of (tile_pair, tile_lam); tile_pair lies in 0 to 15. On lam index l every slot's tile_lam lies in l * 2 to (l + 1) * 2 - 1. Slots from tile_count on are dead and their integrals are ignored; some device has all 8 slots live.
All inputs are finite; a program needn't handle non-finite values.
Results may differ from a plain program's by a relative error of at most 0.0049.
Values may be sent and summed in bfloat16 or wider, within the bound.
No kernel may reach another device: no remote copies, remote signals or barrier semaphores. Data moves between devices by JAX's collectives and lax.ppermute only.
A program may use at most 128 MiB of HBM per device.

v0:
```python
import math
import jax
import jax.numpy as jnp
from jax import lax
from jax.sharding import PartitionSpec as P


def tile_pass(partial_value, tile_group, occ_columns):
    tile_data, pair_list, lam_list, live_total = tile_group
    tile_rows = tile_data.shape[1]
    tile_depth = tile_data.shape[2]

    def add_tile(slot_index, running):
        row_start = pair_list[slot_index] * tile_rows
        occ_rows = lax.dynamic_slice_in_dim(
            occ_columns, lam_list[slot_index] * tile_depth, tile_depth, 0
        )
        contrib = jnp.einsum(
            "rls,lj->jrs", tile_data[slot_index], occ_rows, preferred_element_type=jnp.float32
        )
        current = lax.dynamic_slice_in_dim(running, row_start, tile_rows, 1)
        return lax.dynamic_update_slice_in_dim(running, current + contrib, row_start, 1)

    return lax.fori_loop(0, live_total, add_tile, partial_value)


def on_device(
    integrals, tile_pair, tile_lam, tile_count, mu_index, nu_index, occupied_coef, virtual_coef
):
    lam_count = lax.axis_size("lam")
    pair_count = lax.axis_size("pair")
    occ_total = occupied_coef.shape[1]
    vir_total = virtual_coef.shape[1]
    basis_count = occupied_coef.shape[0]
    rows_here = mu_index.shape[0]
    tile_data = integrals[0]
    pair_list = tile_pair[0]
    lam_list = tile_lam[0]
    live_total = tile_count[0, 0]
    tile_groups = (tile_data, pair_list, lam_list, live_total)
    occ_share = occ_total // lam_count
    partial_value = jnp.zeros((occupied_coef.shape[1], rows_here, basis_count), jnp.float32)
    partial_value = tile_pass(partial_value, tile_groups, occupied_coef)
    summed = lax.psum(partial_value, "lam")
    own_half = lax.dynamic_slice_in_dim(summed, lax.axis_index("lam") * occ_share, occ_share, 0)
    vir_share = vir_total // pair_count
    half_low = own_half.astype(jnp.bfloat16).reshape(occ_share * rows_here, basis_count)
    mixed = jnp.dot(half_low, virtual_coef, preferred_element_type=jnp.float32)
    mixed = mixed.astype(jnp.bfloat16).reshape(occ_share, rows_here, pair_count, vir_share)
    first_all, second_all = (
        lax.all_gather(mu_index, "pair", axis=0, tiled=True),
        lax.all_gather(nu_index, "pair", axis=0, tiled=True),
    )
    received = lax.all_to_all(mixed, "pair", split_axis=2, concat_axis=1, tiled=True)
    item_count = received.shape[0]
    total_rows = received.shape[1]
    column_count = received.shape[3]
    mixed_rows = received.reshape(item_count, total_rows, column_count)
    row_block = math.gcd(total_rows, 256)

    def add_rows(running, row_start):
        occ_rows = jnp.take(
            occupied_coef, lax.dynamic_slice_in_dim(first_all, row_start, row_block), axis=0
        ).astype(jnp.float32)
        vir_rows = jnp.take(
            virtual_coef, lax.dynamic_slice_in_dim(second_all, row_start, row_block), axis=0
        ).astype(jnp.float32)
        weights = (
            (occ_rows[:, :, None] * vir_rows[:, None, :])
            .astype(jnp.bfloat16)
            .reshape(row_block, occ_total * vir_total)
        )
        mixed_piece = lax.dynamic_slice_in_dim(mixed_rows, row_start, row_block, 1)
        return (
            running
            + jnp.einsum("qrb,rk->qbk", mixed_piece, weights, preferred_element_type=jnp.float32),
            None,
        )

    start_total = jnp.zeros((item_count, column_count, occ_total * vir_total), jnp.float32)
    result, _ = lax.scan(
        add_rows, start_total, jnp.arange(0, total_rows, row_block, dtype=jnp.int32)
    )
    return result


def solution(mesh):
    placed = (
        P("pair", "lam", None, None, None),
        P("pair", "lam"),
        P("pair", "lam"),
        P("pair", "lam"),
        P("pair"),
        P("pair"),
        P(),
        P(),
    )
    return jax.shard_map(
        on_device, mesh=mesh, in_specs=placed, out_specs=P("lam", "pair", None), check_vma=False
    )
```

profile of v0, /device:TPU:32, one launch (start us, length us, event | category | flops | bytes accessed | tf_op | source)
XLA Modules:
  0.0 604.5 jit_solution(9514965633434375320)
XLA Ops:
  2.5 27.5 %while.21 = (s32[]{:T(128)}, f32[16,64,1024]{2,1,0:T(8,128)}, s32[]{:T(128)}, s32[8]{0:T(128)S(1)}, s32[8]{0:T(128)S(1)}, /*index=5*/bf16[1024,16]{0,1:T(8,128)(...) while((s32[]{:T(128)}, f32[16,64,1024]{2,1,0:T(8,128)}, ...), condition=%wide.region_1.0_spmd, body=%wide.region_0.0_spmd.sunk | while | flops 8454157 | bytes 2101547 | solution.py:24
  30.1 110.6 %all-reduce.4 = bf16[16,64,1024]{2,1,0:T(8,128)(2,1)} all-reduce(f32[16,64,1024]{2,1,0:T(8,128)} %get-tuple-element.85), channel_id=1, replica_groups=mesh['pair'=32,'lam'=8] {'lam'}, use_global_device_ids=true, to_apply=%region_2.0 | all-reduce | flops 1048576 | bytes 6291456 | tf_op jit(solution)/shard_map/psum | solution.py:44
  145.6 13.8 %all-to-all-start = ((bf16[32,2,2560]{2,1,0:T(2,128)(2,1)}), bf16[32,2,2560]{2,1,0:T(2,128)(2,1)}, u32[]{:S(2)}, u32[]{:S(2)}) async-start(bf16[32,2,2560]{2,1,0:T(2,128)(2,1)} %reshape.99), calls=%async_computation | async-start | bytes 655360 | tf_op jit(solution)/shard_map/all_to_all | solution.py:54
  162.0 128.6 %all-reduce.2 = (s32[2048]{0:T(1024)}, s32[2048]{0:T(1024)}) all-reduce(s32[2048]{0:T(1024)S(1)} %dynamic-update-slice, s32[2048]{0:T(1024)S(1)} %dynamic-update-slice.1), channel_id=1, replica_groups=mesh['pair'=32,'lam'=8] {'pair'}, use_global_device_ids=true, to_apply=%add | all-reduce | flops 4096 | bytes 32768
  293.9 310.6 %while.22 = (s32[]{:T(128)}, f32[2,40,20480]{2,1,0:T(8,128)}, s32[8]{0:T(128)S(1)}, bf16[2,2048,40]{1,2,0:T(8,128)(2,1)}, s32[2048]{0:T(1024)}, /*index=5*/bf16[...) while((s32[]{:T(128)}, f32[2,40,20480]{2,1,0:T(8,128)}, ...), condition=%wide.region_4.5_spmd.clone, body=%wide.region_3.4_spmd.clone.sunk | while | flops 853292032 | bytes 59753956 | solution.py:81
  307.6 14.8 %reshape.110 = bf16[256,20480,1]{1,0,2:T(8,128)(2,1)} reshape(bf16[256,16,1280]{2,1,0:T(8,128)(2,1)} %multiply_convert_fusion.2) | data formatting | bytes 20971520 | tf_op jit(solution)/shard_map/while/body/eval_jaxpr/convert_element_type | solution.py:70
  322.3 8.8 %convolution_add_fusion.5 = f32[2,40,20480]{2,1,0:T(8,128)} fusion(bf16[256,20480,1]{1,0,2:T(8,128)(2,1)} %reshape.110, f32[2,40,20480]{2,1,0:T(8,128)} %get-tuple-element.331, pred[]{:T(512)S(6)} %compare.3, bf16[2,2048,40]{1,2,0:T(8,128)(2,1)} %get-tuple-element.344, s32[]{:T(128)S(6)} %select_n.68), kind=kOutput, calls=%fused_computation.10.clone.1 | convolution fusion | flops 842137600 | bytes 23633924 | tf_op jit(solution)/shard_map/while/body/eval_jaxpr/qrb,rk->qbk/dot_general | solution.py:76
  344.8 14.8 %reshape.110 = bf16[256,20480,1]{1,0,2:T(8,128)(2,1)} reshape(bf16[256,16,1280]{2,1,0:T(8,128)(2,1)} %multiply_convert_fusion.2) | data formatting | bytes 20971520 | tf_op jit(solution)/shard_map/while/body/eval_jaxpr/convert_element_type | solution.py:70
  359.5 10.6 %convolution_add_fusion.5 = f32[2,40,20480]{2,1,0:T(8,128)} fusion(bf16[256,20480,1]{1,0,2:T(8,128)(2,1)} %reshape.110, f32[2,40,20480]{2,1,0:T(8,128)} %get-tuple-element.331, pred[]{:T(512)S(6)} %compare.3, bf16[2,2048,40]{1,2,0:T(8,128)(2,1)} %get-tuple-element.344, s32[]{:T(128)S(6)} %select_n.68), kind=kOutput, calls=%fused_computation.10.clone.1 | convolution fusion | flops 842137600 | bytes 23633924 | tf_op jit(solution)/shard_map/while/body/eval_jaxpr/qrb,rk->qbk/dot_general | solution.py:76
  377.1 6.7 %multiply_convert_fusion.2 = bf16[256,16,1280]{2,1,0:T(8,128)(2,1)} fusion(f32[256,1280]{1,0:T(8,128)} %select_convert_fusion.4, f32[256,16]{1,0:T(8,128)S(1)} %select_convert_fusion.5), kind=kLoop, calls=%fused_computation.11.clone.1 | loop fusion | flops 10485760 | bytes 11812864 | tf_op jit(solution)/shard_map/while/body/eval_jaxpr/convert_element_type | solution.py:70
  383.8 14.8 %reshape.110 = bf16[256,20480,1]{1,0,2:T(8,128)(2,1)} reshape(bf16[256,16,1280]{2,1,0:T(8,128)(2,1)} %multiply_convert_fusion.2) | data formatting | bytes 20971520 | tf_op jit(solution)/shard_map/while/body/eval_jaxpr/convert_element_type | solution.py:70
  398.6 10.6 %convolution_add_fusion.5 = f32[2,40,20480]{2,1,0:T(8,128)} fusion(bf16[256,20480,1]{1,0,2:T(8,128)(2,1)} %reshape.110, f32[2,40,20480]{2,1,0:T(8,128)} %get-tuple-element.331, pred[]{:T(512)S(6)} %compare.3, bf16[2,2048,40]{1,2,0:T(8,128)(2,1)} %get-tuple-element.344, s32[]{:T(128)S(6)} %select_n.68), kind=kOutput, calls=%fused_computation.10.clone.1 | convolution fusion | flops 842137600 | bytes 23633924 | tf_op jit(solution)/shard_map/while/body/eval_jaxpr/qrb,rk->qbk/dot_general | solution.py:76
  422.9 14.8 %reshape.110 = bf16[256,20480,1]{1,0,2:T(8,128)(2,1)} reshape(bf16[256,16,1280]{2,1,0:T(8,128)(2,1)} %multiply_convert_fusion.2) | data formatting | bytes 20971520 | tf_op jit(solution)/shard_map/while/body/eval_jaxpr/convert_element_type | solution.py:70
  437.7 10.6 %convolution_add_fusion.5 = f32[2,40,20480]{2,1,0:T(8,128)} fusion(bf16[256,20480,1]{1,0,2:T(8,128)(2,1)} %reshape.110, f32[2,40,20480]{2,1,0:T(8,128)} %get-tuple-element.331, pred[]{:T(512)S(6)} %compare.3, bf16[2,2048,40]{1,2,0:T(8,128)(2,1)} %get-tuple-element.344, s32[]{:T(128)S(6)} %select_n.68), kind=kOutput, calls=%fused_computation.10.clone.1 | convolution fusion | flops 842137600 | bytes 23633924 | tf_op jit(solution)/shard_map/while/body/eval_jaxpr/qrb,rk->qbk/dot_general | solution.py:76
  455.3 6.7 %multiply_convert_fusion.2 = bf16[256,16,1280]{2,1,0:T(8,128)(2,1)} fusion(f32[256,1280]{1,0:T(8,128)} %select_convert_fusion.4, f32[256,16]{1,0:T(8,128)S(1)} %select_convert_fusion.5), kind=kLoop, calls=%fused_computation.11.clone.1 | loop fusion | flops 10485760 | bytes 11812864 | tf_op jit(solution)/shard_map/while/body/eval_jaxpr/convert_element_type | solution.py:70
  462.0 14.8 %reshape.110 = bf16[256,20480,1]{1,0,2:T(8,128)(2,1)} reshape(bf16[256,16,1280]{2,1,0:T(8,128)(2,1)} %multiply_convert_fusion.2) | data formatting | bytes 20971520 | tf_op jit(solution)/shard_map/while/body/eval_jaxpr/convert_element_type | solution.py:70
  476.7 10.6 %convolution_add_fusion.5 = f32[2,40,20480]{2,1,0:T(8,128)} fusion(bf16[256,20480,1]{1,0,2:T(8,128)(2,1)} %reshape.110, f32[2,40,20480]{2,1,0:T(8,128)} %get-tuple-element.331, pred[]{:T(512)S(6)} %compare.3, bf16[2,2048,40]{1,2,0:T(8,128)(2,1)} %get-tuple-element.344, s32[]{:T(128)S(6)} %select_n.68), kind=kOutput, calls=%fused_computation.10.clone.1 | convolution fusion | flops 842137600 | bytes 23633924 | tf_op jit(solution)/shard_map/while/body/eval_jaxpr/qrb,rk->qbk/dot_general | solution.py:76
  494.3 6.7 %multiply_convert_fusion.2 = bf16[256,16,1280]{2,1,0:T(8,128)(2,1)} fusion(f32[256,1280]{1,0:T(8,128)} %select_convert_fusion.4, f32[256,16]{1,0:T(8,128)S(1)} %select_convert_fusion.5), kind=kLoop, calls=%fused_computation.11.clone.1 | loop fusion | flops 10485760 | bytes 11812864 | tf_op jit(solution)/shard_map/while/body/eval_jaxpr/convert_element_type | solution.py:70
  501.0 14.8 %reshape.110 = bf16[256,20480,1]{1,0,2:T(8,128)(2,1)} reshape(bf16[256,16,1280]{2,1,0:T(8,128)(2,1)} %multiply_convert_fusion.2) | data formatting | bytes 20971520 | tf_op jit(solution)/shard_map/while/body/eval_jaxpr/convert_element_type | solution.py:70
  515.8 10.6 %convolution_add_fusion.5 = f32[2,40,20480]{2,1,0:T(8,128)} fusion(bf16[256,20480,1]{1,0,2:T(8,128)(2,1)} %reshape.110, f32[2,40,20480]{2,1,0:T(8,128)} %get-tuple-element.331, pred[]{:T(512)S(6)} %compare.3, bf16[2,2048,40]{1,2,0:T(8,128)(2,1)} %get-tuple-element.344, s32[]{:T(128)S(6)} %select_n.68), kind=kOutput, calls=%fused_computation.10.clone.1 | convolution fusion | flops 842137600 | bytes 23633924 | tf_op jit(solution)/shard_map/while/body/eval_jaxpr/qrb,rk->qbk/dot_general | solution.py:76
  540.0 14.8 %reshape.110 = bf16[256,20480,1]{1,0,2:T(8,128)(2,1)} reshape(bf16[256,16,1280]{2,1,0:T(8,128)(2,1)} %multiply_convert_fusion.2) | data formatting | bytes 20971520 | tf_op jit(solution)/shard_map/while/body/eval_jaxpr/convert_element_type | solution.py:70
  554.8 10.6 %convolution_add_fusion.5 = f32[2,40,20480]{2,1,0:T(8,128)} fusion(bf16[256,20480,1]{1,0,2:T(8,128)(2,1)} %reshape.110, f32[2,40,20480]{2,1,0:T(8,128)} %get-tuple-element.331, pred[]{:T(512)S(6)} %compare.3, bf16[2,2048,40]{1,2,0:T(8,128)(2,1)} %get-tuple-element.344, s32[]{:T(128)S(6)} %select_n.68), kind=kOutput, calls=%fused_computation.10.clone.1 | convolution fusion | flops 842137600 | bytes 23633924 | tf_op jit(solution)/shard_map/while/body/eval_jaxpr/qrb,rk->qbk/dot_general | solution.py:76
  579.1 14.8 %reshape.110 = bf16[256,20480,1]{1,0,2:T(8,128)(2,1)} reshape(bf16[256,16,1280]{2,1,0:T(8,128)(2,1)} %multiply_convert_fusion.2) | data formatting | bytes 20971520 | tf_op jit(solution)/shard_map/while/body/eval_jaxpr/convert_element_type | solution.py:70
  593.8 10.6 %convolution_add_fusion.5 = f32[2,40,20480]{2,1,0:T(8,128)} fusion(bf16[256,20480,1]{1,0,2:T(8,128)(2,1)} %reshape.110, f32[2,40,20480]{2,1,0:T(8,128)} %get-tuple-element.331, pred[]{:T(512)S(6)} %compare.3, bf16[2,2048,40]{1,2,0:T(8,128)(2,1)} %get-tuple-element.344, s32[]{:T(128)S(6)} %select_n.68), kind=kOutput, calls=%fused_computation.10.clone.1 | convolution fusion | flops 842137600 | bytes 23633924 | tf_op jit(solution)/shard_map/while/body/eval_jaxpr/qrb,rk->qbk/dot_general | solution.py:76
  (152 shorter events, 104.0 us)
Async XLA Ops:
  0.0 2.5 copy-start.1
  0.0 2.5 copy-start.2
  30.1 111.7 %copy-start = (bf16[1024,1280]{1,0:T(8,128)(2,1)S(1)}, bf16[1024,1280]{1,0:T(8,128)(2,1)}, u32[]{:S(2)}) copy-start(bf16[1024,1280]{1,0:T(8,128)(2,1)} %param.19) | copy-start | bytes 7864324
  140.7 19.6 %copy-start.5 = (u32[256]{0:T(256)S(1)}, u32[256]{0:T(256)}, u32[]{:S(2)}) copy-start(u32[256]{0:T(256)} %constant.71) | copy-start | bytes 3076
  140.7 20.7 %copy-start.3 = (s32[64]{0:T(128)S(1)}, s32[64]{0:T(128)}, u32[]{:S(2)}) copy-start(s32[64]{0:T(128)} %param.16) | copy-start | bytes 772
  140.7 21.0 %copy-start.4 = (s32[64]{0:T(128)S(1)}, s32[64]{0:T(128)}, u32[]{:S(2)}) copy-start(s32[64]{0:T(128)} %param.17) | copy-start | bytes 772
  145.6 145.0 %all-to-all-start = ((bf16[32,2,2560]{2,1,0:T(2,128)(2,1)}), bf16[32,2,2560]{2,1,0:T(2,128)(2,1)}, u32[]{:S(2)}, u32[]{:S(2)}) async-start(bf16[32,2,2560]{2,1,0:T(2,128)(2,1)} %reshape.99), calls=%async_computation | async-start | bytes 655360 | tf_op jit(solution)/shard_map/all_to_all | solution.py:54
  293.9 3.5 copy-start.6
  322.3 8.8 %copy-start.7 = (s32[8]{0:T(128)S(1)}, s32[8]{0:T(128)}, u32[]{:S(2)}) copy-start(s32[8]{0:T(128)} %copy-done.6) | copy-start | bytes 100 | tf_op jit(solution)/shard_map/while
  331.1 3.5 copy-start.6
  359.5 10.6 %copy-start.7 = (s32[8]{0:T(128)S(1)}, s32[8]{0:T(128)}, u32[]{:S(2)}) copy-start(s32[8]{0:T(128)} %copy-done.6) | copy-start | bytes 100 | tf_op jit(solution)/shard_map/while
  370.2 3.5 copy-start.6
  398.6 10.6 %copy-start.7 = (s32[8]{0:T(128)S(1)}, s32[8]{0:T(128)}, u32[]{:S(2)}) copy-start(s32[8]{0:T(128)} %copy-done.6) | copy-start | bytes 100 | tf_op jit(solution)/shard_map/while
  409.2 3.5 copy-start.6
  437.7 10.6 %copy-start.7 = (s32[8]{0:T(128)S(1)}, s32[8]{0:T(128)}, u32[]{:S(2)}) copy-start(s32[8]{0:T(128)} %copy-done.6) | copy-start | bytes 100 | tf_op jit(solution)/shard_map/while
  448.3 3.5 copy-start.6
  476.7 10.6 %copy-start.7 = (s32[8]{0:T(128)S(1)}, s32[8]{0:T(128)}, u32[]{:S(2)}) copy-start(s32[8]{0:T(128)} %copy-done.6) | copy-start | bytes 100 | tf_op jit(solution)/shard_map/while
  487.4 3.5 copy-start.6
  515.8 10.6 %copy-start.7 = (s32[8]{0:T(128)S(1)}, s32[8]{0:T(128)}, u32[]{:S(2)}) copy-start(s32[8]{0:T(128)} %copy-done.6) | copy-start | bytes 100 | tf_op jit(solution)/shard_map/while
  526.4 3.5 copy-start.6
  554.8 10.6 %copy-start.7 = (s32[8]{0:T(128)S(1)}, s32[8]{0:T(128)}, u32[]{:S(2)}) copy-start(s32[8]{0:T(128)} %copy-done.6) | copy-start | bytes 100 | tf_op jit(solution)/shard_map/while
  565.4 3.5 copy-start.6
  593.8 10.6 %copy-start.7 = (s32[8]{0:T(128)S(1)}, s32[8]{0:T(128)}, u32[]{:S(2)}) copy-start(s32[8]{0:T(128)} %copy-done.6) | copy-start | bytes 100 | tf_op jit(solution)/shard_map/while
where the time goes:
time: 609 us; the launch traced here: 604 us
  blocking collectives  239 us (39%)
  local copies, waits for them, and re-layouts  166 us (27%)
  matrix products  89.1 us (15%)
  other arithmetic  70.6 us (12%)
  loops' own time  25.5 us (4%)
  starting transfers between devices  13.8 us (2%)
    unnamed x1, blocking collectives  129 us
    convert_element_type x8, local copies, waits for them, and re-layouts, add_rows(): weights = (occ_rows[:, :, None] * vir_rows[:, None, :]).astype(jnp.bfloat...  118 us
    psum x1, blocking collectives, on_device(): summed = lax.psum(partial_value, 'lam')  111 us
    dot_general x8, matrix products, add_rows(): jnp.einsum('qrb,rk->qbk', mixed_piece, weights, preferred_element_type=jn...  83.1 us
    convert_element_type x8, other arithmetic, add_rows(): weights = (occ_rows[:, :, None] * vir_rows[:, None, :]).astype(jnp.bfloat...  53.6 us
    another operation x1, loops' own time, on_device(): lax.scan(add_rows, start_total, jnp.arange(0, total_rows, row_block, dtyp...  16.6 us
    all_to_all x1, starting transfers between devices, on_device(): lax.all_to_all(mixed, 'pair', split_axis=2, concat_axis=1, tiled=True)  13.8 us
  transfers between devices with their start and end apart: 1, of which 0 were waited for; matrix products, arithmetic and copies ran while one was open for 0% of the time, Pallas kernels for 0%

commit v1 on v0

--- a/solution.py
+++ b/solution.py
@@ -1,8 +1,16 @@
+import functools
 import math
 import jax
 import jax.numpy as jnp
 from jax import lax
 from jax.sharding import PartitionSpec as P
+
+
+def state_hold(z_in, axis_id):
+    return lax.all_gather(z_in, axis_id).sum(axis=0)
+
+
+mark_the_orders = functools.partial(state_hold, axis_id="lam")
 
 
 def tile_pass(partial_value, tile_group, occ_columns):
@@ -41,7 +49,7 @@
     occ_share = occ_total // lam_count
     partial_value = jnp.zeros((occupied_coef.shape[1], rows_here, basis_count), jnp.float32)
     partial_value = tile_pass(partial_value, tile_groups, occupied_coef)
-    summed = lax.psum(partial_value, "lam")
+    summed = mark_the_orders(partial_value)
     own_half = lax.dynamic_slice_in_dim(summed, lax.axis_index("lam") * occ_share, occ_share, 0)
     vir_share = vir_total // pair_count
     half_low = own_half.astype(jnp.bfloat16).reshape(occ_share * rows_here, basis_count)

time: 609 us -> 865 us (1.42)
  waiting for transfers between devices: 0.01 us -> 352 us
  blocking collectives: 239 us -> 129 us
  other arithmetic: 70.6 us -> 85 us
  between operations: 0.69 us -> 14.2 us
    all_gather x0 -> x1, waiting for transfers between devices: none -> 352 us  [state_hold(): return lax.all_gather(z_in, axis_id).sum(axis=0)]
    psum x1 -> x0, blocking collectives: 111 us -> none  [on_device(): summed = lax.psum(partial_value, 'lam')]
    reduce_sum x0 -> x1, other arithmetic: none -> 14.3 us  [state_hold(): return lax.all_gather(z_in, axis_id).sum(axis=0)]
  transfers between devices with their start and end apart: 1 -> 2, of which waited for: 0 -> 1; matrix products, arithmetic and copies ran while one was open for 0% -> 0% of each run, Pallas kernels for 0% -> 0%
where the time goes in v1:
time: 865 us; the launch traced here: 860 us
  waiting for transfers between devices  352 us (41%)
  local copies, waits for them, and re-layouts  158 us (18%)
  blocking collectives  129 us (15%)
  matrix products  92 us (11%)
  other arithmetic  85 us (10%)
  loops' own time  23.6 us (3%)
  between operations  14.2 us (2%)
    all_gather x1, waiting for transfers between devices, state_hold(): return lax.all_gather(z_in, axis_id).sum(axis=0)  352 us
    unnamed x1, blocking collectives  129 us
    convert_element_type x8, local copies, waits for them, and re-layouts, add_rows(): weights = (occ_rows[:, :, None] * vir_rows[:, None, :]).astype(jnp.bfloat...  118 us
    dot_general x8, matrix products, add_rows(): jnp.einsum('qrb,rk->qbk', mixed_piece, weights, preferred_element_type=jn...  83.1 us
    convert_element_type x8, other arithmetic, add_rows(): weights = (occ_rows[:, :, None] * vir_rows[:, None, :]).astype(jnp.bfloat...  53.6 us
  transfers between devices with their start and end apart: 2, of which 1 were waited for; matrix products, arithmetic and copies ran while one was open for 0% of the time, Pallas kernels for 0%

profile of v1, /device:TPU:32, one launch (start us, length us, event | category | flops | bytes accessed | tf_op | source)
XLA Modules:
  0.0 860.1 jit_solution(17624780048464373269)
XLA Ops:
  9.1 22.0 %while.21 = (s32[]{:T(128)}, f32[16,64,1024]{2,0,1:T(8,128)}, s32[]{:T(128)}, s32[8]{0:T(128)S(1)}, s32[8]{0:T(128)S(1)}, /*index=5*/bf16[1024,16]{0,1:T(8,128)(...) while((s32[]{:T(128)}, f32[16,64,1024]{2,0,1:T(8,128)}, ...), condition=%wide.region_1.0_spmd, body=%wide.region_0.0_spmd.sunk | while | flops 8454157 | bytes 1052967 | solution.py:32
  31.1 351.6 %all-gather.3.cloned.1.call-done = f32[128,64,1024]{2,0,1:T(8,128)} async-done(((f32[16,64,1024]{2,0,1:T(8,128)}), f32[128,64,1024]{2,0,1:T(8,128)}) %all-gather.3.cloned.1.call-update) | async-done | bytes 33554448 | tf_op jit(solution)/shard_map/all_gather | solution.py:10
  382.7 14.3 %reduce_sum.9 = bf16[16,64,1024]{2,0,1:T(8,128)(2,1)} reduce(f32[8,16,64,1024]{3,1,0,2:T(8,128)} %bitcast.44, f32[]{:T(128)} %constant.51.clone.1), dimensions={0}, to_apply=%region_2.0 | reduce | flops 7340032 | bytes 35651588 | tf_op jit(solution)/shard_map/reduce_sum | solution.py:10
  402.4 7.2 all-to-all-start
  412.5 128.6 %all-reduce.2 = (s32[2048]{0:T(1024)}, s32[2048]{0:T(1024)}) all-reduce(s32[2048]{0:T(1024)S(1)} %dynamic-update-slice, s32[2048]{0:T(1024)S(1)} %dynamic-update-slice.1), channel_id=1, replica_groups=mesh['pair'=32,'lam'=8] {'pair'}, use_global_device_ids=true, to_apply=%add | all-reduce | flops 4096 | bytes 32768
  544.4 308.9 %while.22 = (s32[]{:T(128)}, f32[2,40,20480]{2,1,0:T(8,128)}, s32[8]{0:T(128)S(1)}, bf16[2,2048,40]{1,2,0:T(8,128)(2,1)}, s32[2048]{0:T(1024)}, /*index=5*/bf16[...) while((s32[]{:T(128)}, f32[2,40,20480]{2,1,0:T(8,128)}, ...), condition=%wide.region_4.5_spmd.clone, body=%wide.region_3.4_spmd.clone.sunk | while | flops 853292032 | bytes 59753956 | solution.py:89
  557.8 14.8 %reshape.111 = bf16[256,20480,1]{1,0,2:T(8,128)(2,1)} reshape(bf16[256,16,1280]{2,1,0:T(8,128)(2,1)} %multiply_convert_fusion.2) | data formatting | bytes 20971520 | tf_op jit(solution)/shard_map/while/body/eval_jaxpr/convert_element_type | solution.py:78
  572.6 8.8 %convolution_add_fusion.3 = f32[2,40,20480]{2,1,0:T(8,128)} fusion(bf16[256,20480,1]{1,0,2:T(8,128)(2,1)} %reshape.111, f32[2,40,20480]{2,1,0:T(8,128)} %get-tuple-element.347, pred[]{:T(512)S(6)} %compare.3, bf16[2,2048,40]{1,2,0:T(8,128)(2,1)} %get-tuple-element.360, s32[]{:T(128)S(6)} %select_n.68), kind=kOutput, calls=%fused_computation.9.clone.1 | convolution fusion | flops 842137600 | bytes 23633924 | tf_op jit(solution)/shard_map/while/body/eval_jaxpr/qrb,rk->qbk/dot_general | solution.py:84
  588.1 6.7 multiply_convert_fusion.2
  594.8 14.8 %reshape.111 = bf16[256,20480,1]{1,0,2:T(8,128)(2,1)} reshape(bf16[256,16,1280]{2,1,0:T(8,128)(2,1)} %multiply_convert_fusion.2) | data formatting | bytes 20971520 | tf_op jit(solution)/shard_map/while/body/eval_jaxpr/convert_element_type | solution.py:78
  609.6 10.6 %convolution_add_fusion.3 = f32[2,40,20480]{2,1,0:T(8,128)} fusion(bf16[256,20480,1]{1,0,2:T(8,128)(2,1)} %reshape.111, f32[2,40,20480]{2,1,0:T(8,128)} %get-tuple-element.347, pred[]{:T(512)S(6)} %compare.3, bf16[2,2048,40]{1,2,0:T(8,128)(2,1)} %get-tuple-element.360, s32[]{:T(128)S(6)} %select_n.68), kind=kOutput, calls=%fused_computation.9.clone.1 | convolution fusion | flops 842137600 | bytes 23633924 | tf_op jit(solution)/shard_map/while/body/eval_jaxpr/qrb,rk->qbk/dot_general | solution.py:84
  633.7 14.8 %reshape.111 = bf16[256,20480,1]{1,0,2:T(8,128)(2,1)} reshape(bf16[256,16,1280]{2,1,0:T(8,128)(2,1)} %multiply_convert_fusion.2) | data formatting | bytes 20971520 | tf_op jit(solution)/shard_map/while/body/eval_jaxpr/convert_element_type | solution.py:78
  648.4 10.6 %convolution_add_fusion.3 = f32[2,40,20480]{2,1,0:T(8,128)} fusion(bf16[256,20480,1]{1,0,2:T(8,128)(2,1)} %reshape.111, f32[2,40,20480]{2,1,0:T(8,128)} %get-tuple-element.347, pred[]{:T(512)S(6)} %compare.3, bf16[2,2048,40]{1,2,0:T(8,128)(2,1)} %get-tuple-element.360, s32[]{:T(128)S(6)} %select_n.68), kind=kOutput, calls=%fused_computation.9.clone.1 | convolution fusion | flops 842137600 | bytes 23633924 | tf_op jit(solution)/shard_map/while/body/eval_jaxpr/qrb,rk->qbk/dot_general | solution.py:84
  665.8 6.7 multiply_convert_fusion.2
  672.5 14.8 %reshape.111 = bf16[256,20480,1]{1,0,2:T(8,128)(2,1)} reshape(bf16[256,16,1280]{2,1,0:T(8,128)(2,1)} %multiply_convert_fusion.2) | data formatting | bytes 20971520 | tf_op jit(solution)/shard_map/while/body/eval_jaxpr/convert_element_type | solution.py:78
  687.3 10.6 %convolution_add_fusion.3 = f32[2,40,20480]{2,1,0:T(8,128)} fusion(bf16[256,20480,1]{1,0,2:T(8,128)(2,1)} %reshape.111, f32[2,40,20480]{2,1,0:T(8,128)} %get-tuple-element.347, pred[]{:T(512)S(6)} %compare.3, bf16[2,2048,40]{1,2,0:T(8,128)(2,1)} %get-tuple-element.360, s32[]{:T(128)S(6)} %select_n.68), kind=kOutput, calls=%fused_computation.9.clone.1 | convolution fusion | flops 842137600 | bytes 23633924 | tf_op jit(solution)/shard_map/while/body/eval_jaxpr/qrb,rk->qbk/dot_general | solution.py:84
  711.4 14.8 %reshape.111 = bf16[256,20480,1]{1,0,2:T(8,128)(2,1)} reshape(bf16[256,16,1280]{2,1,0:T(8,128)(2,1)} %multiply_convert_fusion.2) | data formatting | bytes 20971520 | tf_op jit(solution)/shard_map/while/body/eval_jaxpr/convert_element_type | solution.py:78
  726.1 10.6 %convolution_add_fusion.3 = f32[2,40,20480]{2,1,0:T(8,128)} fusion(bf16[256,20480,1]{1,0,2:T(8,128)(2,1)} %reshape.111, f32[2,40,20480]{2,1,0:T(8,128)} %get-tuple-element.347, pred[]{:T(512)S(6)} %compare.3, bf16[2,2048,40]{1,2,0:T(8,128)(2,1)} %get-tuple-element.360, s32[]{:T(128)S(6)} %select_n.68), kind=kOutput, calls=%fused_computation.9.clone.1 | convolution fusion | flops 842137600 | bytes 23633924 | tf_op jit(solution)/shard_map/while/body/eval_jaxpr/qrb,rk->qbk/dot_general | solution.py:84
  750.2 14.8 %reshape.111 = bf16[256,20480,1]{1,0,2:T(8,128)(2,1)} reshape(bf16[256,16,1280]{2,1,0:T(8,128)(2,1)} %multiply_convert_fusion.2) | data formatting | bytes 20971520 | tf_op jit(solution)/shard_map/while/body/eval_jaxpr/convert_element_type | solution.py:78
  765.0 10.6 %convolution_add_fusion.3 = f32[2,40,20480]{2,1,0:T(8,128)} fusion(bf16[256,20480,1]{1,0,2:T(8,128)(2,1)} %reshape.111, f32[2,40,20480]{2,1,0:T(8,128)} %get-tuple-element.347, pred[]{:T(512)S(6)} %compare.3, bf16[2,2048,40]{1,2,0:T(8,128)(2,1)} %get-tuple-element.360, s32[]{:T(128)S(6)} %select_n.68), kind=kOutput, calls=%fused_computation.9.clone.1 | convolution fusion | flops 842137600 | bytes 23633924 | tf_op jit(solution)/shard_map/while/body/eval_jaxpr/qrb,rk->qbk/dot_general | solution.py:84
  789.0 14.8 %reshape.111 = bf16[256,20480,1]{1,0,2:T(8,128)(2,1)} reshape(bf16[256,16,1280]{2,1,0:T(8,128)(2,1)} %multiply_convert_fusion.2) | data formatting | bytes 20971520 | tf_op jit(solution)/shard_map/while/body/eval_jaxpr/convert_element_type | solution.py:78
  803.8 10.6 %convolution_add_fusion.3 = f32[2,40,20480]{2,1,0:T(8,128)} fusion(bf16[256,20480,1]{1,0,2:T(8,128)(2,1)} %reshape.111, f32[2,40,20480]{2,1,0:T(8,128)} %get-tuple-element.347, pred[]{:T(512)S(6)} %compare.3, bf16[2,2048,40]{1,2,0:T(8,128)(2,1)} %get-tuple-element.360, s32[]{:T(128)S(6)} %select_n.68), kind=kOutput, calls=%fused_computation.9.clone.1 | convolution fusion | flops 842137600 | bytes 23633924 | tf_op jit(solution)/shard_map/while/body/eval_jaxpr/qrb,rk->qbk/dot_general | solution.py:84
  827.8 14.8 %reshape.111 = bf16[256,20480,1]{1,0,2:T(8,128)(2,1)} reshape(bf16[256,16,1280]{2,1,0:T(8,128)(2,1)} %multiply_convert_fusion.2) | data formatting | bytes 20971520 | tf_op jit(solution)/shard_map/while/body/eval_jaxpr/convert_element_type | solution.py:78
  842.6 10.6 %convolution_add_fusion.3 = f32[2,40,20480]{2,1,0:T(8,128)} fusion(bf16[256,20480,1]{1,0,2:T(8,128)(2,1)} %reshape.111, f32[2,40,20480]{2,1,0:T(8,128)} %get-tuple-element.347, pred[]{:T(512)S(6)} %compare.3, bf16[2,2048,40]{1,2,0:T(8,128)(2,1)} %get-tuple-element.360, s32[]{:T(128)S(6)} %select_n.68), kind=kOutput, calls=%fused_computation.9.clone.1 | convolution fusion | flops 842137600 | bytes 23633924 | tf_op jit(solution)/shard_map/while/body/eval_jaxpr/qrb,rk->qbk/dot_general | solution.py:84
  (148 shorter events, 105.9 us)
Async XLA Ops:
  6.5 2.5 copy-start.1
  6.5 2.5 copy-start.2
  6.5 376.1 %all-gather.3.cloned.1.call-start = ((), (), s32[]{:S(2)}) async-start(), calls=%async_computation.1 | async-start | bytes 37748736 | tf_op jit(solution)/shard_map/all_gather | solution.py:10
  382.7 15.9 %copy-start = (bf16[1024,1280]{1,0:T(8,128)(2,1)S(1)}, bf16[1024,1280]{1,0:T(8,128)(2,1)}, u32[]{:S(2)}) copy-start(bf16[1024,1280]{1,0:T(8,128)(2,1)} %param.19) | copy-start | bytes 7864324
  397.0 13.6 %copy-start.5 = (u32[256]{0:T(256)S(1)}, u32[256]{0:T(256)}, u32[]{:S(2)}) copy-start(u32[256]{0:T(256)} %constant.72) | copy-start | bytes 3076
  397.0 15.0 %copy-start.3 = (s32[64]{0:T(128)S(1)}, s32[64]{0:T(128)}, u32[]{:S(2)}) copy-start(s32[64]{0:T(128)} %param.16) | copy-start | bytes 772
  397.0 15.2 %copy-start.4 = (s32[64]{0:T(128)S(1)}, s32[64]{0:T(128)}, u32[]{:S(2)}) copy-start(s32[64]{0:T(128)} %param.17) | copy-start | bytes 772
  402.4 138.6 %all-to-all-start = ((bf16[32,2,2560]{2,1,0:T(2,128)(2,1)}), bf16[32,2,2560]{2,1,0:T(2,128)(2,1)}, u32[]{:S(2)}, u32[]{:S(2)}) async-start(bf16[32,2,2560]{2,1,0:T(2,128)(2,1)} %reshape.100), calls=%async_computation | async-start | bytes 655360 | tf_op jit(solution)/shard_map/all_to_all | solution.py:62
  544.4 3.3 copy-start.6
  572.6 8.8 %copy-start.7 = (s32[8]{0:T(128)S(1)}, s32[8]{0:T(128)}, u32[]{:S(2)}) copy-start(s32[8]{0:T(128)} %copy-done.6) | copy-start | bytes 100 | tf_op jit(solution)/shard_map/while
  581.4 3.3 copy-start.6
  609.6 10.6 %copy-start.7 = (s32[8]{0:T(128)S(1)}, s32[8]{0:T(128)}, u32[]{:S(2)}) copy-start(s32[8]{0:T(128)} %copy-done.6) | copy-start | bytes 100 | tf_op jit(solution)/shard_map/while
  620.2 3.3 copy-start.6
  648.4 10.6 %copy-start.7 = (s32[8]{0:T(128)S(1)}, s32[8]{0:T(128)}, u32[]{:S(2)}) copy-start(s32[8]{0:T(128)} %copy-done.6) | copy-start | bytes 100 | tf_op jit(solution)/shard_map/while
  659.1 3.3 copy-start.6
  687.3 10.6 %copy-start.7 = (s32[8]{0:T(128)S(1)}, s32[8]{0:T(128)}, u32[]{:S(2)}) copy-start(s32[8]{0:T(128)} %copy-done.6) | copy-start | bytes 100 | tf_op jit(solution)/shard_map/while
  697.9 3.3 copy-start.6
  726.1 10.6 %copy-start.7 = (s32[8]{0:T(128)S(1)}, s32[8]{0:T(128)}, u32[]{:S(2)}) copy-start(s32[8]{0:T(128)} %copy-done.6) | copy-start | bytes 100 | tf_op jit(solution)/shard_map/while
  736.8 3.3 copy-start.6
  765.0 10.6 %copy-start.7 = (s32[8]{0:T(128)S(1)}, s32[8]{0:T(128)}, u32[]{:S(2)}) copy-start(s32[8]{0:T(128)} %copy-done.6) | copy-start | bytes 100 | tf_op jit(solution)/shard_map/while
  775.6 3.3 copy-start.6
  803.8 10.6 %copy-start.7 = (s32[8]{0:T(128)S(1)}, s32[8]{0:T(128)}, u32[]{:S(2)}) copy-start(s32[8]{0:T(128)} %copy-done.6) | copy-start | bytes 100 | tf_op jit(solution)/shard_map/while
  814.4 3.3 copy-start.6
  842.6 10.6 %copy-start.7 = (s32[8]{0:T(128)S(1)}, s32[8]{0:T(128)}, u32[]{:S(2)}) copy-start(s32[8]{0:T(128)} %copy-done.6) | copy-start | bytes 100 | tf_op jit(solution)/shard_map/while
Sparse Core Ops, SparseCore 0:
  31.2 351.4 all-gather.2
